TPU v7x, 512 devices: a whole 4x4x16 slice. The times are simulated.
512 devices in a mesh: dp: 8 (over x, core), expert: 64 (over y, z).
Axes of the slice: x: 4, y: 4, z: 16, core: 2. Of those that a mesh axis runs over, the one named last changes fastest.
Arguments:
- tokens: bfloat16 [65536, 1024], P(('dp', 'expert')), may hold values from -6 to 6
- grad_out: bfloat16 [65536, 1024], P(('dp', 'expert')), may hold values from -6 to 6
- expert_ids: int32 [65536, 8], P(('dp', 'expert')), may hold values from 0 to 63, all different within a row; in each aligned block of 128 rows (0 to 127, 128 to 255, ...) at most 18 rows name the same one
- gates: float32 [65536, 8], P(('dp', 'expert')), may hold values from 0.1 to 0.5
- w_in: bfloat16 [64, 1024, 768], P('expert', 'dp'), may hold values from -0.1875 to 0.1875
- w_down: bfloat16 [64, 384, 1024], P('expert', 'dp'), may hold values from -0.3125 to 0.3125
Outputs:
- grad_tokens: bfloat16 [65536, 1024], P(('dp', 'expert'))
- grad_in: float32 [64, 1024, 768], P('expert', 'dp')
- grad_down: float32 [64, 384, 1024], P('expert', 'dp')
Inputs may be any that keep to these rules, and one draw needn't show every extreme that they name: `expert_ids`: each token names 8 different experts; among the tokens of one device no expert is named more than 18 times, a bound that some block reaches.
All inputs are finite; a program needn't handle non-finite values.
Results may differ from a plain program's by a relative error of at most 0.015.
Values may be sent and summed in bfloat16 or wider, within the bound.
No kernel may reach another device: no remote copies, remote signals or barrier semaphores. Data moves between devices by JAX's collectives and lax.ppermute only.
A program may use at most 64 MiB of HBM per device.

v0:
```python
import jax
import jax.numpy as jnp
from jax import lax
from jax.sharding import Mesh
from jax.sharding import PartitionSpec as P


def hidden_from(preact):
    half_width = preact.shape[1] // 2
    gate_pre = preact[:, :half_width]
    up_pre = preact[:, half_width:]
    sigmoid_gate = jax.nn.sigmoid(gate_pre)
    return (gate_pre * sigmoid_gate * up_pre).astype(jnp.bfloat16)


def pre_grads(preact, grad_hidden):
    half_width = preact.shape[1] // 2
    gate_pre = preact[:, :half_width]
    up_pre = preact[:, half_width:]
    sigmoid_gate = jax.nn.sigmoid(gate_pre)
    grad_gate = grad_hidden * up_pre * sigmoid_gate * (1.0 + gate_pre * (1.0 - sigmoid_gate))
    grad_up = grad_hidden * gate_pre * sigmoid_gate
    return jnp.concatenate([grad_gate, grad_up], axis=1).astype(jnp.bfloat16)


def contract_first(left, right):
    return lax.dot_general(
        left, right, (((0,), (0,)), ((), ())), preferred_element_type=jnp.float32
    )


def contract_last(left, right):
    return lax.dot_general(
        left, right, (((1,), (1,)), ((), ())), preferred_element_type=jnp.float32
    )


def expert_exchange(blocks, rows, cols):
    capacity, width = (blocks.shape[1], blocks.shape[2])
    blocks = blocks.reshape(rows, cols, capacity, width)
    blocks = lax.all_to_all(blocks, "ez", 1, 1, tiled=True)
    blocks = lax.all_to_all(blocks, "ey", 0, 0, tiled=True)
    return blocks.reshape(rows * cols, capacity, width)


def on_device(tokens, grad_out, expert_ids, gates, w_in, w_down):
    token_rows, model_width = tokens.shape
    route_width = expert_ids.shape[1]
    rows = lax.axis_size("ey")
    cols = lax.axis_size("ez")
    expert_count = rows * cols
    route_total = token_rows * route_width
    capacity = route_total // expert_count + max(1, route_total // (8 * expert_count))
    slot_total = expert_count * capacity
    flat_ids = expert_ids.reshape(route_total)
    route_marks = (flat_ids[:, None] == jnp.arange(expert_count, dtype=jnp.int32)[None, :]).astype(
        jnp.int32
    )
    route_index = jnp.arange(route_total, dtype=jnp.int32)
    lower_table = (route_index[None, :] <= route_index[:, None]).astype(jnp.bfloat16)
    running = jnp.dot(
        lower_table, route_marks.astype(jnp.bfloat16), preferred_element_type=jnp.float32
    )
    slot_ranks = jnp.sum((running.astype(jnp.int32) - 1) * route_marks, axis=1)
    targets = (flat_ids * capacity + slot_ranks).reshape(token_rows, route_width)
    slot_index = jnp.arange(slot_total, dtype=jnp.int32)
    slot_hits = targets[None, :, :] == slot_index[:, None, None]
    slot_of_token = jnp.any(slot_hits, axis=2).astype(jnp.bfloat16)
    slot_gates = jnp.sum(jnp.where(slot_hits, gates[None, :, :], 0.0), axis=(1, 2))
    send_tokens = jnp.dot(slot_of_token, tokens, preferred_element_type=jnp.float32).astype(
        jnp.bfloat16
    )
    picked_grads = jnp.dot(slot_of_token, grad_out, preferred_element_type=jnp.float32)
    send_grads = (slot_gates[:, None] * picked_grads).astype(jnp.bfloat16)
    send_both = jnp.concatenate([send_tokens, send_grads], axis=1)
    recv_both = expert_exchange(
        send_both.reshape(expert_count, capacity, 2 * model_width), rows, cols
    ).reshape(slot_total, 2 * model_width)
    slot_tokens = recv_both[:, :model_width]
    slot_grads = recv_both[:, model_width:]
    local_in = w_in[0]
    local_down = w_down[0]
    full_in, full_down = (
        lax.all_gather(local_in, "dp", axis=0, tiled=True),
        lax.all_gather(local_down, "dp", axis=0, tiled=True),
    )
    preact = jnp.dot(slot_tokens, full_in, preferred_element_type=jnp.float32)
    grad_hidden = contract_last(slot_grads, full_down)
    pre_grad = pre_grads(preact, grad_hidden)
    slot_back = contract_last(pre_grad, full_in).astype(jnp.bfloat16)
    hidden_act = hidden_from(preact)
    grad_in_local = lax.psum_scatter(
        contract_first(slot_tokens, pre_grad).astype(jnp.bfloat16),
        "dp",
        scatter_dimension=0,
        tiled=True,
    ).astype(jnp.float32)
    grad_down_local = lax.psum_scatter(
        contract_first(hidden_act, slot_grads).astype(jnp.bfloat16),
        "dp",
        scatter_dimension=0,
        tiled=True,
    ).astype(jnp.float32)
    slot_return = expert_exchange(
        slot_back.reshape(expert_count, capacity, model_width), rows, cols
    ).reshape(slot_total, model_width)
    grad_tokens = contract_first(slot_of_token, slot_return).astype(jnp.bfloat16)
    return (grad_tokens, grad_in_local[None], grad_down_local[None])


def solution(mesh):
    dp_size = mesh.shape["dp"]
    expert_devices = mesh.devices.reshape(dp_size, -1)
    rows = 4 if expert_devices.shape[1] % 4 == 0 else 1
    split_mesh = Mesh(
        expert_devices.reshape(dp_size, rows, expert_devices.shape[1] // rows), ("dp", "ey", "ez")
    )
    token_spec = P(("dp", "ey", "ez"), None)
    weight_spec = P(("ey", "ez"), "dp", None)
    in_specs = (token_spec, token_spec, token_spec, token_spec, weight_spec, weight_spec)
    out_specs = (token_spec, weight_spec, weight_spec)
    return jax.shard_map(
        on_device, mesh=split_mesh, in_specs=in_specs, out_specs=out_specs, check_vma=False
    )
```

profile of v0, /device:TPU:38, one launch (start us, length us, event | category | flops | bytes accessed | tf_op | source)
XLA Modules:
  0.0 530.4 jit_solution(8605643046941876970)
XLA Ops:
  7.2 0.0 copy-start
  7.2 0.8 copy.38
  8.0 0.1 eq.28
  8.1 0.0 copy-start.3
  8.1 0.6 fusion.22
  8.7 0.1 reduce_sum.21
  8.9 0.7 multiply_add_fusion
  9.6 4.2 fusion
  13.8 9.3 %select_reduce_fusion = f32[1152]{0:T(1024)S(1)} fusion(f32[128,8]{0,1:T(8,128)} %param.9, s32[128,8]{0,1:T(8,128)S(1)} %multiply_add_fusion), kind=kLoop, calls=%fused_computation.2 | loop fusion | flops 3537792 | bytes 12800 | tf_op jit(solution)/shard_map/reduce_sum | solution.py:69
  23.1 0.0 copy-done
  23.1 0.8 convolution_convert_fusion.1
  23.9 0.0 copy-done.3
  23.9 0.8 fusion.2
  24.8 2.5 pad_maximum_fusion
  27.3 6.8 %copy.40 = bf16[1152,2048]{1,0:T(8,128)(2,1)} copy(bf16[1152,2048]{0,1:T(8,128)(2,1)} %pad_maximum_fusion) | data formatting | bytes 9437184 | tf_op jit(solution)/shard_map/concatenate | solution.py:75
  34.1 7.6 %reshape_reshape.12 = bf16[4,16,18,2048]{3,2,1,0:T(8,128)(2,1)} reshape(bf16[1152,2048]{1,0:T(8,128)(2,1)} %copy.40) | data formatting | bytes 9437184 | tf_op jit(solution)/shard_map/reshape;reshape | solution.py:40
  41.7 6.8 %copy.41 = bf16[4,16,18,2048]{3,0,2,1:T(4,128)(2,1)S(1)} copy(bf16[4,16,18,2048]{3,2,1,0:T(8,128)(2,1)} %reshape_reshape.12) | data formatting | bytes 9437184 | tf_op jit(solution)/shard_map/reshape;reshape | solution.py:40
  48.5 223.2 %all_to_all.20 = bf16[4,16,18,2048]{3,0,2,1:T(4,128)(2,1)S(1)} all-to-all(bf16[4,16,18,2048]{3,0,2,1:T(4,128)(2,1)S(1)} %copy.41), channel_id=1, replica_groups=mesh['dp'=8,'ey'=4,'ez'=16] {'ez'}, dimensions={1} | all-to-all | bytes 9437184 | tf_op jit(solution)/shard_map/all_to_all | solution.py:41
  271.7 4.7 copy.42
  276.4 0.0 copy-start.4
  276.4 5.1 all-to-all-start.1
  281.5 0.0 all-gather.4.cloned.1.call-start
  281.6 0.7 all-gather.4.cloned.1.call-update
  282.2 0.0 copy-done.4
  282.3 13.4 %all-gather = bf16[1,384,1024]{2,1,0:T(8,128)(2,1)S(1)} all-gather(bf16[1,48,1024]{2,1,0:T(8,128)(2,1)S(1)} %copy-done.4), channel_id=2, replica_groups=mesh['dp'=8,'ey'=4,'ez'=16] {'dp'}, dimensions={1}, use_global_device_ids=true | all-gather | bytes 884736 | tf_op jit(solution)/shard_map/all_gather | solution.py:85
  295.6 36.4 %all-to-all-done.1 = bf16[4,16,18,2048]{3,1,2,0:T(8,128)(2,1)} async-done(((bf16[4,16,18,2048]{3,1,2,0:T(8,128)(2,1)}), bf16[4,16,18,2048]{3,1,2,0:T(8,128)(2,1)}, u32[]{:S(2)}, u32[]{:S(2)}) %all-to-all-start.1) | async-done | bytes 4718624 | tf_op jit(solution)/shard_map/all_to_all | solution.py:42
  332.1 7.9 %copy.43 = bf16[4,16,18,2048]{3,2,1,0:T(8,128)(2,1)} copy(bf16[4,16,18,2048]{3,1,2,0:T(8,128)(2,1)} %all-to-all-done.1) | data formatting | bytes 9437184 | tf_op jit(solution)/shard_map/all_to_all | solution.py:42
  340.0 7.7 %reshape_reshape.13 = bf16[1152,2048]{1,0:T(8,128)(2,1)} reshape(bf16[4,16,18,2048]{3,2,1,0:T(8,128)(2,1)} %copy.43) | data formatting | bytes 9437184 | tf_op jit(solution)/shard_map/reshape;reshape | solution.py:78
  347.8 0.0 all-gather.4.cloned.1.call-done
  347.8 0.0 copy-start.2
  347.8 4.6 fusion.5
  352.4 0.0 copy-done.2
  352.4 0.0 copy-start.6
  352.4 0.0 copy-start.5
  352.4 1.6 multiply_convert_fusion.2
  354.1 0.2 copy-done.6
  354.3 0.0 copy-start.7
  354.3 0.0 copy-start.8
  354.3 0.9 copy-done.7
  355.2 0.3 copy-done.8
  355.5 0.0 copy-done.5
  355.5 3.5 convolution_convert_fusion
  359.1 2.7 reshape_reshape.14
  361.8 3.4 copy.44
  365.2 11.2 %all-to-all-start.2 = ((bf16[4,16,18,1024]{3,0,2,1:T(4,128)(2,1)}), bf16[4,16,18,1024]{3,0,2,1:T(4,128)(2,1)S(1)}, u32[]{:S(2)}, u32[]{:S(2)}) async-start(bf16[4,16,18,1024]{3,0,2,1:T(4,128)(2,1)} %copy.44), calls=%async_computation.2 | async-start | bytes 4718592 | tf_op jit(solution)/shard_map/all_to_all | solution.py:41
  376.4 0.0 reduce-scatter.5.cloned.1.call-start
  376.4 4.9 fusion.16
  381.3 0.0 reduce-scatter.5.cloned.1.call-update
  381.3 0.3 reduce-scatter.3.cloned.1.call-start
  381.6 5.6 %fusion.11 = bf16[1024,768]{1,0:T(8,128)(2,1)} fusion(bf16[1152,2048]{1,0:T(8,128)(2,1)} %reshape_reshape.13, bf16[1152,384]{0,1:T(8,128)(2,1)} %copy-done.8, bf16[1152,384]{0,1:T(8,128)(2,1)} %copy-done.7), kind=kOutput, calls=%fused_computation.23 | convolution fusion | flops 1816264704 | bytes 5701632 | tf_op jit(solution)/shard_map/dot_general | solution.py:27
  387.2 0.0 reduce-scatter.3.cloned.1.call-update
  387.2 92.5 %all-to-all-done.2 = bf16[4,16,18,1024]{3,0,2,1:T(4,128)(2,1)S(1)} async-done(((bf16[4,16,18,1024]{3,0,2,1:T(4,128)(2,1)}), bf16[4,16,18,1024]{3,0,2,1:T(4,128)(2,1)S(1)}, u32[]{:S(2)}, u32[]{:S(2)}) %all-to-all-start.2) | async-done | bytes 2359328 | tf_op jit(solution)/shard_map/all_to_all | solution.py:41
  479.7 2.7 copy.45
  482.5 4.5 all-to-all-start.3
  487.0 0.0 reduce-scatter.5.cloned.1.call-done
  487.0 1.6 bitcast_convert_fusion.1
  488.6 0.0 reduce-scatter.3.cloned.1.call-done
  488.6 1.7 bitcast_convert_fusion
  490.3 25.3 %all-to-all-done.3 = bf16[4,16,18,1024]{3,1,2,0:T(8,128)(2,1)} async-done(((bf16[4,16,18,1024]{3,1,2,0:T(8,128)(2,1)}), bf16[4,16,18,1024]{3,1,2,0:T(8,128)(2,1)}, u32[]{:S(2)}, u32[]{:S(2)}) %all-to-all-start.3) | async-done | bytes 2359328 | tf_op jit(solution)/shard_map/all_to_all | solution.py:42
  515.6 3.1 copy.46
  518.7 0.0 copy-start.1
  518.7 2.2 reshape_reshape.15
  520.9 2.9 convolution_convert_fusion.2
  523.8 0.0 copy-done.1
  (1 shorter events, 0.0 us)
Async XLA Ops:
  7.2 15.9 %copy-start = (bf16[128,1024]{1,0:T(8,128)(2,1)S(1)}, bf16[128,1024]{1,0:T(8,128)(2,1)}, u32[]{:S(2)}) copy-start(bf16[128,1024]{1,0:T(8,128)(2,1)} %param.6) | copy-start | bytes 786436
  8.1 15.8 %copy-start.3 = (bf16[128,1024]{1,0:T(8,128)(2,1)S(1)}, bf16[128,1024]{1,0:T(8,128)(2,1)}, u32[]{:S(2)}) copy-start(bf16[128,1024]{1,0:T(8,128)(2,1)} %param.7) | copy-start | bytes 786436
  276.4 5.8 %copy-start.4 = (bf16[1,48,1024]{2,1,0:T(8,128)(2,1)S(1)}, bf16[1,48,1024]{2,1,0:T(8,128)(2,1)}, u32[]{:S(2)}) copy-start(bf16[1,48,1024]{2,1,0:T(8,128)(2,1)} %param.11) | copy-start | bytes 294916
  276.4 55.7 %all-to-all-start.1 = ((bf16[4,16,18,2048]{3,1,2,0:T(8,128)(2,1)}), bf16[4,16,18,2048]{3,1,2,0:T(8,128)(2,1)}, u32[]{:S(2)}, u32[]{:S(2)}) async-start(bf16[4,16,18,2048]{3,1,2,0:T(8,128)(2,1)} %copy.42), calls=%async_computation.1 | async-start | bytes 9437184 | tf_op jit(solution)/shard_map/all_to_all | solution.py:42
  281.5 66.2 %all-gather.4.cloned.1.call-start = ((), (), s32[]{:S(2)}) async-start(), calls=%async_computation.8 | async-start | bytes 1769472 | tf_op jit(solution)/shard_map/all_gather | solution.py:84
  347.8 4.7 copy-start.2
  352.4 1.9 copy-start.6
  352.4 3.1 copy-start.5
  354.3 0.9 copy-start.7
  354.3 1.2 copy-start.8
  365.2 114.5 %all-to-all-start.2 = ((bf16[4,16,18,1024]{3,0,2,1:T(4,128)(2,1)}), bf16[4,16,18,1024]{3,0,2,1:T(4,128)(2,1)S(1)}, u32[]{:S(2)}, u32[]{:S(2)}) async-start(bf16[4,16,18,1024]{3,0,2,1:T(4,128)(2,1)} %copy.44), calls=%async_computation.2 | async-start | bytes 4718592 | tf_op jit(solution)/shard_map/all_to_all | solution.py:41
  376.4 110.6 %reduce-scatter.5.cloned.1.call-start = ((), (), s32[]{:S(2)}) async-start(), calls=%async_computation.7 | async-start | bytes 884736 | tf_op jit(solution)/shard_map/reduce_scatter | solution.py:98
  381.3 107.3 %reduce-scatter.3.cloned.1.call-start = ((), (), s32[]{:S(2)}) async-start(), calls=%async_computation.6 | async-start | bytes 1769472 | tf_op jit(solution)/shard_map/reduce_scatter | solution.py:92
  482.5 33.1 %all-to-all-start.3 = ((bf16[4,16,18,1024]{3,1,2,0:T(8,128)(2,1)}), bf16[4,16,18,1024]{3,1,2,0:T(8,128)(2,1)}, u32[]{:S(2)}, u32[]{:S(2)}) async-start(bf16[4,16,18,1024]{3,1,2,0:T(8,128)(2,1)} %copy.45), calls=%async_computation.3 | async-start | bytes 4718592 | tf_op jit(solution)/shard_map/all_to_all | solution.py:42
  518.7 5.2 copy-start.1
Sparse Core Ops, SparseCore 0:
  284.4 26.4 all-gather.3
  381.4 35.7 reduce-scatter.4
  420.1 40.1 reduce-scatter.2
where the time goes:
time: 532 us; the launch traced here: 530 us
  blocking collectives  237 us (45%)
  waiting for transfers between devices  155 us (29%)
  local copies, waits for them, and re-layouts  58.2 us (11%)
  matrix products  25.5 us (5%)
  starting transfers between devices  21.1 us (4%)
  other arithmetic  20.1 us (4%)
  between operations  13.9 us (3%)
    all_to_all x1, blocking collectives, expert_exchange(): blocks = lax.all_to_all(blocks, 'ez', 1, 1, tiled=True)  223 us
    all_to_all x1, waiting for transfers between devices, expert_exchange(): blocks = lax.all_to_all(blocks, 'ez', 1, 1, tiled=True)  92.5 us
    all_to_all x2, waiting for transfers between devices, expert_exchange(): blocks = lax.all_to_all(blocks, 'ey', 0, 0, tiled=True)  61.8 us
    another operation x4, local copies, waits for them, and re-layouts, expert_exchange(): blocks = blocks.reshape(rows, cols, capacity, width)  20.5 us
    dot_general x3, matrix products, contract_first(): lax.dot_general(left, right, (((0,), (0,)), ((), ())), preferred_element_...  13.4 us
    all_gather x1, blocking collectives, on_device(): lax.all_gather(local_down, 'dp', axis=0, tiled=True)  13.4 us
    all_to_all x1, starting transfers between devices, expert_exchange(): blocks = lax.all_to_all(blocks, 'ez', 1, 1, tiled=True)  11.2 us
    all_to_all x2, local copies, waits for them, and re-layouts, expert_exchange(): blocks = lax.all_to_all(blocks, 'ey', 0, 0, tiled=True)  11 us
  transfers between devices with their start and end apart: 6, of which 3 were waited for; matrix products, arithmetic and copies ran while one was open for 6% of the time, Pallas kernels for 0%

commit v1 on v0

--- a/solution.py
+++ b/solution.py
@@ -82,7 +82,9 @@
     local_down = w_down[0]
     full_in, full_down = (
         lax.all_gather(local_in, "dp", axis=0, tiled=True),
-        lax.all_gather(local_down, "dp", axis=0, tiled=True),
+        jnp.concatenate(
+            lax.all_to_all(jnp.stack([local_down] * lax.axis_size("dp")), "dp", 0, 0), axis=0
+        ),
     )
     preact = jnp.dot(slot_tokens, full_in, preferred_element_type=jnp.float32)
     grad_hidden = contract_last(slot_grads, full_down)

time: 532 us -> 543 us (1.021)
  the two profiles are of different devices: /device:TPU:38 before, /device:TPU:32 now
where the time goes in v1:
time: 543 us; the launch traced here: 542 us
  blocking collectives  223 us (41%)
  waiting for transfers between devices  170 us (31%)
  local copies, waits for them, and re-layouts  59.2 us (11%)
  matrix products  29.9 us (6%)
  starting transfers between devices  25.4 us (5%)
  other arithmetic  20.1 us (4%)
  between operations  13.9 us (3%)
    all_to_all x1, blocking collectives, expert_exchange(): blocks = lax.all_to_all(blocks, 'ez', 1, 1, tiled=True)  223 us
    all_to_all x1, waiting for transfers between devices, expert_exchange(): blocks = lax.all_to_all(blocks, 'ez', 1, 1, tiled=True)  94 us
    all_to_all x2, waiting for transfers between devices, expert_exchange(): blocks = lax.all_to_all(blocks, 'ey', 0, 0, tiled=True)  75.5 us
    another operation x4, local copies, waits for them, and re-layouts, expert_exchange(): blocks = blocks.reshape(rows, cols, capacity, width)  20.6 us
    dot_general x3, matrix products, contract_first(): lax.dot_general(left, right, (((0,), (0,)), ((), ())), preferred_element_...  13.4 us
    all_to_all x1, starting transfers between devices, expert_exchange(): blocks = lax.all_to_all(blocks, 'ez', 1, 1, tiled=True)  11.2 us
    all_to_all x2, local copies, waits for them, and re-layouts, expert_exchange(): blocks = lax.all_to_all(blocks, 'ey', 0, 0, tiled=True)  11 us
  transfers between devices with their start and end apart: 7, of which 3 were waited for; matrix products, arithmetic and copies ran while one was open for 7% of the time, Pallas kernels for 0%

profile of v1, /device:TPU:32, one launch (start us, length us, event | category | flops | bytes accessed | tf_op | source)
XLA Modules:
  0.0 541.9 jit_solution(4121309988977753090)
XLA Ops:
  7.2 0.0 copy-start
  7.2 0.8 copy.38
  8.0 0.1 eq.28
  8.1 0.0 copy-start.2
  8.1 0.6 fusion.22
  8.7 0.1 reduce_sum.21
  8.9 0.7 multiply_add_fusion
  9.6 4.2 fusion
  13.8 9.3 %select_reduce_fusion = f32[1152]{0:T(1024)S(1)} fusion(f32[128,8]{0,1:T(8,128)} %param.9, s32[128,8]{0,1:T(8,128)S(1)} %multiply_add_fusion), kind=kLoop, calls=%fused_computation.2 | loop fusion | flops 3537792 | bytes 12800 | tf_op jit(solution)/shard_map/reduce_sum | solution.py:69
  23.1 0.0 copy-done
  23.1 0.8 convolution_convert_fusion.1
  23.9 0.0 copy-done.2
  23.9 0.8 fusion.2
  24.8 2.5 pad_maximum_fusion
  27.3 6.8 %copy.40 = bf16[1152,2048]{1,0:T(8,128)(2,1)} copy(bf16[1152,2048]{0,1:T(8,128)(2,1)} %pad_maximum_fusion) | data formatting | bytes 9437184 | tf_op jit(solution)/shard_map/concatenate | solution.py:75
  34.1 7.6 %reshape_reshape.12 = bf16[4,16,18,2048]{3,2,1,0:T(8,128)(2,1)} reshape(bf16[1152,2048]{1,0:T(8,128)(2,1)} %copy.40) | data formatting | bytes 9437184 | tf_op jit(solution)/shard_map/reshape;reshape | solution.py:40
  41.7 6.8 %copy.41 = bf16[4,16,18,2048]{3,0,2,1:T(4,128)(2,1)S(1)} copy(bf16[4,16,18,2048]{3,2,1,0:T(8,128)(2,1)} %reshape_reshape.12) | data formatting | bytes 9437184 | tf_op jit(solution)/shard_map/reshape;reshape | solution.py:40
  48.5 223.2 %all_to_all.25 = bf16[4,16,18,2048]{3,0,2,1:T(4,128)(2,1)S(1)} all-to-all(bf16[4,16,18,2048]{3,0,2,1:T(4,128)(2,1)S(1)} %copy.41), channel_id=1, replica_groups=mesh['dp'=8,'ey'=4,'ez'=16] {'ez'}, dimensions={1} | all-to-all | bytes 9437184 | tf_op jit(solution)/shard_map/all_to_all | solution.py:41
  271.7 4.8 copy.42
  276.5 0.0 copy-start.3
  276.5 5.1 all-to-all-start.1
  281.6 0.0 all-gather.3.cloned.1.call-start
  281.7 0.7 all-gather.3.cloned.1.call-update
  282.4 49.8 %all-to-all-done.1 = bf16[4,16,18,2048]{3,1,2,0:T(8,128)(2,1)} async-done(((bf16[4,16,18,2048]{3,1,2,0:T(8,128)(2,1)}), bf16[4,16,18,2048]{3,1,2,0:T(8,128)(2,1)}, u32[]{:S(2)}, u32[]{:S(2)}) %all-to-all-start.1) | async-done | bytes 4718624 | tf_op jit(solution)/shard_map/all_to_all | solution.py:42
  332.2 0.0 copy-done.3
  332.2 1.0 stack.3
  333.2 4.3 all-to-all-start.2
  337.5 7.9 %copy.43 = bf16[4,16,18,2048]{3,2,1,0:T(8,128)(2,1)} copy(bf16[4,16,18,2048]{3,1,2,0:T(8,128)(2,1)} %all-to-all-done.1) | data formatting | bytes 9437184 | tf_op jit(solution)/shard_map/all_to_all | solution.py:42
  345.4 7.7 %reshape_reshape.13 = bf16[1152,2048]{1,0:T(8,128)(2,1)} reshape(bf16[4,16,18,2048]{3,2,1,0:T(8,128)(2,1)} %copy.43) | data formatting | bytes 9437184 | tf_op jit(solution)/shard_map/reshape;reshape | solution.py:78
  353.1 0.0 all-gather.3.cloned.1.call-done
  353.1 6.2 %fusion.5 = f32[1152,768]{0,1:T(8,128)} fusion(bf16[1152,2048]{1,0:T(8,128)(2,1)} %reshape_reshape.13, bf16[1,1024,768]{2,1,0:T(8,128)(2,1)} %all-gather.3.cloned.1.call-done), kind=kOutput, calls=%fused_computation.12 | convolution fusion | flops 1811939328 | bytes 7471104 | tf_op jit(solution)/shard_map/dot_general | solution.py:89
  359.4 0.0 all-to-all-done.2
  359.4 0.0 copy-start.4
  359.4 4.4 multiply_convert_fusion.2
  363.8 0.0 copy-start.5
  363.8 0.0 copy-start.6
  363.8 0.9 copy-done.5
  364.7 0.3 copy-done.6
  365.0 0.0 copy-done.4
  365.0 3.6 convolution_convert_fusion
  368.6 2.7 reshape_reshape.14
  371.3 3.5 copy.44
  374.8 11.2 %all-to-all-start.3 = ((bf16[4,16,18,1024]{3,0,2,1:T(4,128)(2,1)}), bf16[4,16,18,1024]{3,0,2,1:T(4,128)(2,1)S(1)}, u32[]{:S(2)}, u32[]{:S(2)}) async-start(bf16[4,16,18,1024]{3,0,2,1:T(4,128)(2,1)} %copy.44), calls=%async_computation.3 | async-start | bytes 4718592 | tf_op jit(solution)/shard_map/all_to_all | solution.py:41
  386.0 0.3 reduce-scatter.5.cloned.1.call-start
  386.3 4.9 fusion.16
  391.1 0.0 reduce-scatter.5.cloned.1.call-update
  391.2 0.0 reduce-scatter.3.cloned.1.call-start
  391.2 5.6 %fusion.11 = bf16[1024,768]{1,0:T(8,128)(2,1)} fusion(bf16[1152,2048]{1,0:T(8,128)(2,1)} %reshape_reshape.13, bf16[1152,384]{0,1:T(8,128)(2,1)} %copy-done.6, bf16[1152,384]{0,1:T(8,128)(2,1)} %copy-done.5), kind=kOutput, calls=%fused_computation.23 | convolution fusion | flops 1816264704 | bytes 5701632 | tf_op jit(solution)/shard_map/dot_general | solution.py:27
  396.8 0.0 reduce-scatter.3.cloned.1.call-update
  396.9 94.0 %all-to-all-done.3 = bf16[4,16,18,1024]{3,0,2,1:T(4,128)(2,1)S(1)} async-done(((bf16[4,16,18,1024]{3,0,2,1:T(4,128)(2,1)}), bf16[4,16,18,1024]{3,0,2,1:T(4,128)(2,1)S(1)}, u32[]{:S(2)}, u32[]{:S(2)}) %all-to-all-start.3) | async-done | bytes 2359328 | tf_op jit(solution)/shard_map/all_to_all | solution.py:41
  490.9 2.7 copy.45
  493.6 4.5 all-to-all-start.4
  498.1 0.0 reduce-scatter.5.cloned.1.call-done
  498.1 1.6 bitcast_convert_fusion.1
  499.7 0.0 reduce-scatter.3.cloned.1.call-done
  499.7 1.7 bitcast_convert_fusion
  501.4 25.7 %all-to-all-done.4 = bf16[4,16,18,1024]{3,1,2,0:T(8,128)(2,1)} async-done(((bf16[4,16,18,1024]{3,1,2,0:T(8,128)(2,1)}), bf16[4,16,18,1024]{3,1,2,0:T(8,128)(2,1)}, u32[]{:S(2)}, u32[]{:S(2)}) %all-to-all-start.4) | async-done | bytes 2359328 | tf_op jit(solution)/shard_map/all_to_all | solution.py:42
  527.1 3.1 copy.46
  530.2 0.0 copy-start.1
  530.2 2.2 reshape_reshape.15
  532.4 2.9 convolution_convert_fusion.2
  535.3 0.0 copy-done.1
  (1 shorter events, 0.0 us)
Async XLA Ops:
  7.2 15.9 %copy-start = (bf16[128,1024]{1,0:T(8,128)(2,1)S(1)}, bf16[128,1024]{1,0:T(8,128)(2,1)}, u32[]{:S(2)}) copy-start(bf16[128,1024]{1,0:T(8,128)(2,1)} %param.6) | copy-start | bytes 786436
  8.1 15.8 %copy-start.2 = (bf16[128,1024]{1,0:T(8,128)(2,1)S(1)}, bf16[128,1024]{1,0:T(8,128)(2,1)}, u32[]{:S(2)}) copy-start(bf16[128,1024]{1,0:T(8,128)(2,1)} %param.7) | copy-start | bytes 786436
  276.5 55.7 %copy-start.3 = (bf16[1,48,1024]{2,1,0:T(8,128)(2,1)S(1)}, bf16[1,48,1024]{2,1,0:T(8,128)(2,1)}, u32[]{:S(2)}) copy-start(bf16[1,48,1024]{2,1,0:T(8,128)(2,1)} %param.11) | copy-start | bytes 294916
  276.5 55.7 %all-to-all-start.1 = ((bf16[4,16,18,2048]{3,1,2,0:T(8,128)(2,1)}), bf16[4,16,18,2048]{3,1,2,0:T(8,128)(2,1)}, u32[]{:S(2)}, u32[]{:S(2)}) async-start(bf16[4,16,18,2048]{3,1,2,0:T(8,128)(2,1)} %copy.42), calls=%async_computation.1 | async-start | bytes 9437184 | tf_op jit(solution)/shard_map/all_to_all | solution.py:42
  281.6 71.5 %all-gather.3.cloned.1.call-start = ((), (), s32[]{:S(2)}) async-start(), calls=%async_computation.9 | async-start | bytes 1769472 | tf_op jit(solution)/shard_map/all_gather | solution.py:84
  333.2 26.2 %all-to-all-start.2 = ((bf16[8,48,1024]{2,1,0:T(8,128)(2,1)}), bf16[8,48,1024]{2,1,0:T(8,128)(2,1)S(1)}, u32[]{:S(2)}, u32[]{:S(2)}) async-start(bf16[8,48,1024]{2,1,0:T(8,128)(2,1)} %stack.3), calls=%async_computation.2 | async-start | bytes 1572864 | tf_op jit(solution)/shard_map/all_to_all | solution.py:86
  359.4 5.6 %copy-start.4 = (bf16[1,1024,768]{2,1,0:T(8,128)(2,1)S(1)}, bf16[1,1024,768]{2,1,0:T(8,128)(2,1)}, u32[]{:S(2)}) copy-start(bf16[1,1024,768]{2,1,0:T(8,128)(2,1)} %all-gather.3.cloned.1.call-done) | copy-start | bytes 4718596
  363.8 0.9 copy-start.5
  363.8 1.2 copy-start.6
  374.8 116.1 %all-to-all-start.3 = ((bf16[4,16,18,1024]{3,0,2,1:T(4,128)(2,1)}), bf16[4,16,18,1024]{3,0,2,1:T(4,128)(2,1)S(1)}, u32[]{:S(2)}, u32[]{:S(2)}) async-start(bf16[4,16,18,1024]{3,0,2,1:T(4,128)(2,1)} %copy.44), calls=%async_computation.3 | async-start | bytes 4718592 | tf_op jit(solution)/shard_map/all_to_all | solution.py:41
  386.0 112.2 %reduce-scatter.5.cloned.1.call-start = ((), (), s32[]{:S(2)}) async-start(), calls=%async_computation.8 | async-start | bytes 884736 | tf_op jit(solution)/shard_map/reduce_scatter | solution.py:100
  391.2 108.5 %reduce-scatter.3.cloned.1.call-start = ((), (), s32[]{:S(2)}) async-start(), calls=%async_computation.7 | async-start | bytes 1769472 | tf_op jit(solution)/shard_map/reduce_scatter | solution.py:94
  493.6 33.5 %all-to-all-start.4 = ((bf16[4,16,18,1024]{3,1,2,0:T(8,128)(2,1)}), bf16[4,16,18,1024]{3,1,2,0:T(8,128)(2,1)}, u32[]{:S(2)}, u32[]{:S(2)}) async-start(bf16[4,16,18,1024]{3,1,2,0:T(8,128)(2,1)} %copy.45), calls=%async_computation.4 | async-start | bytes 4718592 | tf_op jit(solution)/shard_map/all_to_all | solution.py:42
  530.2 5.2 copy-start.1
Sparse Core Ops, SparseCore 0:
  284.5 28.0 all-gather.2
  391.3 39.2 reduce-scatter.4
  433.4 40.3 reduce-scatter.2
